TPU v7x, 256 devices: a whole 4x4x8 slice. The times are simulated.
256 devices in a mesh: section: 4 (over x_lo, core), dp: 8 (over y, x_hi), expert: 8 (over z).
Axes of the slice: x: 4 (x_hi: 2, x_lo: 2; x = x_hi * 2 + x_lo), y: 4, z: 8, core: 2. Of those that a mesh axis runs over, the one named last changes fastest.
Arguments:
- incoming: bfloat16 [4, 2, 1024, 3584], P('section', None, ('dp', 'expert')), may hold values from -6 to 6
- stash: bfloat16 [4, 2, 1024, 3584], P('section', None, ('dp', 'expert')), may hold values from -6 to 6
- expert_ids: int32 [4, 2, 1024, 2], P('section', None, ('dp', 'expert')), may hold values from 0 to 7, all different within a row; in each aligned block of 16 rows (0 to 15, 16 to 31, ..., all dimensions but the last counted through in order) at most 6 rows name the same one
- route_weight: float32 [4, 2, 1024, 2], P('section', None, ('dp', 'expert')), may hold values from 0.1 to 1
- w_gate: bfloat16 [4, 8, 3584, 2048], P('section', 'expert', None, 'dp'), may hold values from -0.09375 to 0.09375
- w_up: bfloat16 [4, 8, 3584, 2048], P('section', 'expert', None, 'dp'), may hold values from -0.09375 to 0.09375
- w_down: bfloat16 [4, 8, 2048, 3584], P('section', 'expert', 'dp'), may hold values from -0.125 to 0.125
Outputs:
- input_grad: bfloat16 [4, 2, 1024, 3584], P('section', None, ('dp', 'expert'))
- grad_gate: bfloat16 [4, 8, 3584, 2048], P('section', 'expert', None, 'dp')
- grad_up: bfloat16 [4, 8, 3584, 2048], P('section', 'expert', None, 'dp')
- grad_down: bfloat16 [4, 8, 2048, 3584], P('section', 'expert', 'dp')
Inputs may be any that keep to these rules, and one draw needn't show every extreme that they name: `expert_ids`: each token names 2 different experts. Among the 16 tokens of one device in one micro-batch (aligned blocks of rows), no expert is named by more than 6 of them, a bound that some block reaches.
All inputs are finite; a program needn't handle non-finite values.
Results may differ from a plain program's by a relative error of at most 0.01.
Values may be sent and summed in bfloat16 or wider, within the bound.
No kernel may reach another device: no remote copies, remote signals or barrier semaphores. Data moves between devices by JAX's collectives and lax.ppermute only.
A program may use at most 128 MiB of HBM per device.

v0:
```python
import jax
import jax.numpy as jnp
from jax import lax
from jax.sharding import PartitionSpec as P


def passed_along(x, axis, by):
    length = lax.axis_size(axis)
    return lax.ppermute(x, axis, [(i, (i + by) % length) for i in range(length)])


def slice_backward(pair_inputs, pair_scaled, gate_slice, up_slice, down_slice):
    contract_rows = (((0,), (0,)), ((), ()))
    contract_last = (((1,), (1,)), ((), ()))
    gate_pre = jnp.dot(pair_inputs, gate_slice, preferred_element_type=jnp.float32)
    up_pre = jnp.dot(pair_inputs, up_slice, preferred_element_type=jnp.float32)
    logistic = jax.nn.sigmoid(gate_pre)
    activated = gate_pre * logistic
    hidden = (activated * up_pre).astype(jnp.bfloat16)
    hidden_grad = lax.dot_general(
        pair_scaled, down_slice, contract_last, preferred_element_type=jnp.float32
    )
    gate_grad = (hidden_grad * up_pre * logistic * (1.0 + gate_pre * (1.0 - logistic))).astype(
        jnp.bfloat16
    )
    up_grad = (hidden_grad * activated).astype(jnp.bfloat16)
    down_total = lax.dot_general(
        hidden, pair_scaled, contract_rows, preferred_element_type=jnp.float32
    )
    gate_total = lax.dot_general(
        pair_inputs, gate_grad, contract_rows, preferred_element_type=jnp.float32
    )
    up_total = lax.dot_general(
        pair_inputs, up_grad, contract_rows, preferred_element_type=jnp.float32
    )
    partial_back = lax.dot_general(
        gate_grad, gate_slice, contract_last, preferred_element_type=jnp.float32
    )
    partial_back = partial_back + lax.dot_general(
        up_grad, up_slice, contract_last, preferred_element_type=jnp.float32
    )
    return (partial_back, gate_total, up_total, down_total)


def per_device(incoming, stash, expert_ids, route_weight, w_gate, w_up, w_down):
    arrived = passed_along(incoming, "section", -1)
    upstream = arrived[0]
    tokens = stash[0]
    mbatch, tok_rows, model_width = tokens.shape
    top_count = expert_ids.shape[-1]
    experts = lax.axis_size("expert")
    capacity = max(2, 3 * tok_rows * top_count // (2 * experts))
    pair_count = tok_rows * top_count
    slot_count = experts * capacity
    chosen = expert_ids[0].reshape(mbatch, pair_count)
    onehot = (chosen[:, :, None] == jnp.arange(experts, dtype=jnp.int32)[None, None, :]).astype(
        jnp.int32
    )
    running = jnp.cumsum(onehot, axis=1) - 1
    position = jnp.sum(onehot * running, axis=2)
    slot_index = chosen * capacity + position
    pair_slot = slot_index[:, :, None] == jnp.arange(slot_count, dtype=jnp.int32)[None, None, :]
    token_slot = pair_slot.reshape(mbatch, tok_rows, top_count, slot_count).any(axis=2)
    token_slot = token_slot.astype(jnp.bfloat16)
    weight_pairs = route_weight[0].reshape(mbatch, pair_count)
    slot_weight = jnp.sum(jnp.where(pair_slot, weight_pairs[:, :, None], 0.0), axis=1)

    def to_slots(rows):
        gathered = jnp.einsum("mts,mtd->msd", token_slot, rows, preferred_element_type=jnp.float32)
        return gathered

    def by_expert(slots):
        return (
            slots.reshape(mbatch, experts, capacity, model_width)
            .transpose(1, 0, 2, 3)
            .reshape(experts, mbatch * capacity, model_width)
        )

    input_slots = by_expert(to_slots(tokens).astype(jnp.bfloat16))
    sent_inputs = lax.all_to_all(input_slots, "expert", 0, 0, tiled=True)
    recv_inputs = lax.all_gather(sent_inputs, "dp", axis=0, tiled=True)
    scaled_slots = by_expert((slot_weight[:, :, None] * to_slots(upstream)).astype(jnp.bfloat16))
    sent_scaled = lax.all_to_all(scaled_slots, "expert", 0, 0, tiled=True)
    recv_scaled = lax.all_gather(sent_scaled, "dp", axis=0, tiled=True)
    input_rows = recv_inputs.reshape(-1, model_width)
    scaled_rows = recv_scaled.reshape(-1, model_width)
    gate_slice = w_gate[0, 0]
    up_slice = w_up[0, 0]
    down_slice = w_down[0, 0]
    partial_rows, gate_total, up_total, down_total = slice_backward(
        input_rows, scaled_rows, gate_slice, up_slice, down_slice
    )
    sent_back = partial_rows.astype(jnp.bfloat16).reshape(recv_inputs.shape)
    summed = lax.psum_scatter(sent_back, "dp", scatter_dimension=0, tiled=True)
    returned = lax.all_to_all(summed, "expert", 0, 0, tiled=True)
    back_slots = (
        returned.reshape(experts, mbatch, capacity, model_width)
        .transpose(1, 0, 2, 3)
        .reshape(mbatch, slot_count, model_width)
    )
    pair_sum = jnp.einsum(
        "mts,msd->mtd", token_slot, back_slots, preferred_element_type=jnp.float32
    )
    input_grad = (upstream.astype(jnp.float32) + pair_sum).astype(jnp.bfloat16)
    grad_gate = gate_total.astype(jnp.bfloat16)[None, None]
    grad_up = up_total.astype(jnp.bfloat16)[None, None]
    grad_down = down_total.astype(jnp.bfloat16)[None, None]
    return (input_grad[None], grad_gate, grad_up, grad_down)


def solution(mesh):
    return jax.shard_map(
        per_device,
        mesh=mesh,
        in_specs=(
            P("section", None, ("dp", "expert"), None),
            P("section", None, ("dp", "expert"), None),
            P("section", None, ("dp", "expert"), None),
            P("section", None, ("dp", "expert"), None),
            P("section", "expert", None, "dp"),
            P("section", "expert", None, "dp"),
            P("section", "expert", "dp", None),
        ),
        out_specs=(
            P("section", None, ("dp", "expert"), None),
            P("section", "expert", None, "dp"),
            P("section", "expert", None, "dp"),
            P("section", "expert", "dp", None),
        ),
        check_vma=False,
    )
```

profile of v0, /device:TPU:1, one launch (start us, length us, event | category | flops | bytes accessed | tf_op | source)
XLA Modules:
  0.0 409.8 jit_solution(17382456177079624147)
XLA Ops:
  9.5 1.3 convolution_convert_fusion.3
  11.9 33.6 %all_to_all.15 = bf16[8,12,3584]{2,1,0:T(8,128)(2,1)S(1)} all-to-all(bf16[8,12,3584]{2,1,0:T(8,128)(2,1)S(1)} %copy.69), channel_id=1, replica_groups=mesh['section'=4,'dp'=8,'expert'=8] {'expert'}, dimensions={0} | all-to-all | bytes 1376256 | tf_op jit(solution)/shard_map/all_to_all | solution.py:80
  46.8 2.1 collective-permute-start
  49.3 4.5 %collective-permute-done = bf16[1,2,16,3584]{3,2,1,0:T(8,128)(2,1)S(1)} collective-permute-done((bf16[1,2,16,3584]{3,2,1,0:T(8,128)(2,1)S(1)}, bf16[1,2,16,3584]{3,2,1,0:T(8,128)(2,1)S(1)}, u32[]{:S(2)}, u32[]{:S(2)}) %collective-permute-start) | collective-permute-done | bytes 229408 | tf_op jit(solution)/shard_map/ppermute | solution.py:9
  55.2 27.8 %all_to_all.16 = bf16[8,12,3584]{2,1,0:T(8,128)(2,1)S(1)} all-to-all(bf16[8,12,3584]{2,1,0:T(8,128)(2,1)S(1)} %copy.64), channel_id=1, replica_groups=mesh['section'=4,'dp'=8,'expert'=8] {'expert'}, dimensions={0} | all-to-all | bytes 1376256 | tf_op jit(solution)/shard_map/all_to_all | solution.py:83
  84.3 46.7 %all-gather.5.cloned.1.call-done = bf16[64,12,3584]{2,0,1:T(8,128)(2,1)} async-done(((bf16[8,12,3584]{2,0,1:T(8,128)(2,1)}), bf16[64,12,3584]{2,0,1:T(8,128)(2,1)}) %all-gather.5.cloned.1.call-update) | async-done | bytes 5505040 | tf_op jit(solution)/shard_map/all_gather | solution.py:81
  131.0 8.6 %copy.71 = bf16[64,12,3584]{2,1,0:T(8,128)(2,1)} copy(bf16[64,12,3584]{2,0,1:T(8,128)(2,1)} %all-gather.5.cloned.1.call-done) | data formatting | bytes 11010048 | tf_op jit(solution)/shard_map/all_gather | solution.py:81
  139.6 9.4 %reshape.58 = bf16[768,3584]{1,0:T(8,128)(2,1)} reshape(bf16[64,12,3584]{2,1,0:T(8,128)(2,1)} %copy.71) | data formatting | bytes 11010048 | tf_op jit(solution)/shard_map/reshape | solution.py:85
  149.1 4.3 %fusion.6 = f32[768,256]{1,0:T(8,128)S(1)} fusion(bf16[768,3584]{1,0:T(8,128)(2,1)} %reshape.58, bf16[1,1,3584,256]{3,2,1,0:T(8,128)(2,1)S(1)} %copy-done), kind=kOutput, calls=%fused_computation.12 | convolution fusion | flops 1409286144 | bytes 8126464 | tf_op jit(solution)/shard_map/dot_general | solution.py:15
  153.8 2.5 fusion.9
  156.3 62.9 %all-gather.3.cloned.1.call-done = bf16[64,12,3584]{2,0,1:T(8,128)(2,1)} async-done(((bf16[8,12,3584]{2,0,1:T(8,128)(2,1)}), bf16[64,12,3584]{2,0,1:T(8,128)(2,1)}) %all-gather.3.cloned.1.call-update) | async-done | bytes 5505040 | tf_op jit(solution)/shard_map/all_gather | solution.py:84
  219.2 8.6 %copy.66 = bf16[64,12,3584]{2,1,0:T(8,128)(2,1)} copy(bf16[64,12,3584]{2,0,1:T(8,128)(2,1)} %all-gather.3.cloned.1.call-done) | data formatting | bytes 11010048 | tf_op jit(solution)/shard_map/all_gather | solution.py:84
  227.8 9.3 %reshape.55 = bf16[768,3584]{1,0:T(8,128)(2,1)} reshape(bf16[64,12,3584]{2,1,0:T(8,128)(2,1)} %copy.66) | data formatting | bytes 11010048 | tf_op jit(solution)/shard_map/reshape | solution.py:86
  237.2 5.0 %multiply_convert_fusion.1 = (bf16[768,256]{1,0:T(8,128)(2,1)S(1)}, bf16[768,256]{1,0:T(8,128)(2,1)S(1)}) fusion(f32[768,256]{1,0:T(8,128)S(1)} %fusion.6, f32[768,256]{1,0:T(8,128)} %fusion.9, bf16[768,3584]{1,0:T(8,128)(2,1)} %reshape.55, bf16[1,1,256,3584]{3,2,1,0:T(8,128)(2,1)} %param.13), kind=kOutput, calls=%fused_computation.20 | convolution fusion | flops 1411842048 | bytes 9699328 | tf_op jit(solution)/shard_map/dot_general | solution.py:20
  242.2 1.6 fusion.4
  244.0 4.0 add_convert_fusion
  248.0 9.2 %reshape.59 = bf16[64,12,3584]{2,1,0:T(8,128)(2,1)} reshape(bf16[768,3584]{1,0:T(8,128)(2,1)} %add_convert_fusion) | data formatting | bytes 11010048 | tf_op jit(solution)/shard_map/reshape | solution.py:93
  257.3 109.4 %reduce-scatter.2.cloned.1.call-done = bf16[8,12,3584]{2,1,0:T(8,128)(2,1)} async-done(((bf16[64,12,3584]{2,1,0:T(8,128)(2,1)}), bf16[8,12,3584]{2,1,0:T(8,128)(2,1)}) %reduce-scatter.2.cloned.1.call-update) | async-done | bytes 688144 | tf_op jit(solution)/shard_map/reduce_scatter | solution.py:94
  366.7 6.9 %all-to-all-start.2 = ((bf16[8,12,3584]{2,1,0:T(8,128)(2,1)}), bf16[8,12,3584]{2,1,0:T(8,128)(2,1)}, u32[]{:S(2)}, u32[]{:S(2)}) async-start(bf16[8,12,3584]{2,1,0:T(8,128)(2,1)} %reduce-scatter.2.cloned.1.call-done), calls=%async_computation.3 | async-start | bytes 1835008 | tf_op jit(solution)/shard_map/all_to_all | solution.py:95
  373.6 5.7 %fusion.1 = bf16[1,1,3584,256]{3,2,1,0:T(8,128)(2,1)} fusion(bf16[768,3584]{1,0:T(8,128)(2,1)} %reshape.58, bf16[768,256]{1,0:T(8,128)(2,1)} %copy-done.6), kind=kOutput, calls=%fused_computation.5 | convolution fusion | flops 1410203648 | bytes 7733248 | tf_op jit(solution)/shard_map/dot_general | solution.py:33
  379.3 2.9 fusion
  382.2 2.9 fusion.2
  385.1 14.9 %all-to-all-done.2 = bf16[8,12,3584]{2,1,0:T(8,128)(2,1)} async-done(((bf16[8,12,3584]{2,1,0:T(8,128)(2,1)}), bf16[8,12,3584]{2,1,0:T(8,128)(2,1)}, u32[]{:S(2)}, u32[]{:S(2)}) %all-to-all-start.2) | async-done | bytes 688160 | tf_op jit(solution)/shard_map/all_to_all | solution.py:95
  400.0 1.6 copy.72
  (64 shorter events, 9.9 us)
Async XLA Ops:
  7.2 141.9 %copy-start = (bf16[1,1,3584,256]{3,2,1,0:T(8,128)(2,1)S(1)}, bf16[1,1,3584,256]{3,2,1,0:T(8,128)(2,1)}, u32[]{:S(2)}) copy-start(bf16[1,1,3584,256]{3,2,1,0:T(8,128)(2,1)} %param.11) | copy-start | bytes 5505028
  7.2 39.7 %copy-start.8 = (bf16[1,2,16,3584]{3,2,1,0:T(8,128)(2,1)S(1)}, bf16[1,2,16,3584]{3,2,1,0:T(8,128)(2,1)}, u32[]{:S(2)}) copy-start(bf16[1,2,16,3584]{3,2,1,0:T(8,128)(2,1)} %param.7) | copy-start | bytes 688132
  7.2 41.8 %copy-start.7 = (f32[1,2,16,2]{2,3,1,0:T(2,128)S(1)}, f32[1,2,16,2]{2,3,1,0:T(2,128)}, u32[]{:S(2)}) copy-start(f32[1,2,16,2]{2,3,1,0:T(2,128)} %param.10) | copy-start | bytes 772
  7.2 123.8 %all-gather.5.cloned.1.call-start = ((), (), s32[]{:S(2)}) async-start(), calls=%async_computation.5 | async-start | bytes 6193152 | tf_op jit(solution)/shard_map/all_gather | solution.py:81
  46.8 172.4 %all-gather.3.cloned.1.call-start = ((), (), s32[]{:S(2)}) async-start(), calls=%async_computation.4 | async-start | bytes 6193152 | tf_op jit(solution)/shard_map/all_gather | solution.py:84
  46.8 6.9 %collective-permute-start = (bf16[1,2,16,3584]{3,2,1,0:T(8,128)(2,1)S(1)}, bf16[1,2,16,3584]{3,2,1,0:T(8,128)(2,1)S(1)}, u32[]{:S(2)}, u32[]{:S(2)}) collective-permute-start(bf16[1,2,16,3584]{3,2,1,0:T(8,128)(2,1)S(1)} %copy-done.8), channel_id=1, source_target_pairs={{0,192},{64,0},{128,64},{192,128},{1,193},{65,1},{129,65},{193,129... | collective-permute-start | bytes 688136 | tf_op jit(solution)/shard_map/ppermute | solution.py:9
  84.2 282.4 %reduce-scatter.2.cloned.1.call-start = ((), (), s32[]{:S(2)}) async-start(), calls=%async_computation.6 | async-start | bytes 8257536 | tf_op jit(solution)/shard_map/reduce_scatter | solution.py:94
  149.1 4.3 %copy-start.1 = (bf16[768,3584]{1,0:T(8,128)(2,1)S(1)}, bf16[768,3584]{1,0:T(8,128)(2,1)}, u32[]{:S(2)}) copy-start(bf16[768,3584]{1,0:T(8,128)(2,1)} %reshape.58) | copy-start | bytes 16515076
  149.1 4.8 %copy-start.2 = (bf16[1,1,3584,256]{3,2,1,0:T(8,128)(2,1)S(1)}, bf16[1,1,3584,256]{3,2,1,0:T(8,128)(2,1)}, u32[]{:S(2)}) copy-start(bf16[1,1,3584,256]{3,2,1,0:T(8,128)(2,1)} %param.12) | copy-start | bytes 5505028
  153.8 83.3 %copy-start.9 = (f32[768,256]{1,0:T(8,128)}, f32[768,256]{1,0:T(8,128)S(1)}, u32[]{:S(2)}) copy-start(f32[768,256]{1,0:T(8,128)S(1)} %fusion.6) | copy-start | bytes 2359300
  242.1 1.7 copy-start.4
  242.2 1.7 copy-start.6
  242.2 1.8 copy-start.3
  366.7 12.6 %slice-start = ((s8[5505024]{0:T(1024)(128)(4,1)}), s8[1310720]{0:T(1024)(128)(4,1)S(1)}, s32[]{:S(2)}) async-start(s8[5505024]{0:T(1024)(128)(4,1)} %bitcast.61), calls=%async_computation.7 | async-start | bytes 2621440
  366.7 33.4 %all-to-all-start.2 = ((bf16[8,12,3584]{2,1,0:T(8,128)(2,1)}), bf16[8,12,3584]{2,1,0:T(8,128)(2,1)}, u32[]{:S(2)}, u32[]{:S(2)}) async-start(bf16[8,12,3584]{2,1,0:T(8,128)(2,1)} %reduce-scatter.2.cloned.1.call-done), calls=%async_computation.3 | async-start | bytes 1835008 | tf_op jit(solution)/shard_map/all_to_all | solution.py:95
  373.5 5.7 %slice-start.1 = ((s8[5505024]{0:T(1024)(128)(4,1)}), s8[4194304]{0:T(1024)(128)(4,1)S(1)}, s32[]{:S(2)}) async-start(s8[5505024]{0:T(1024)(128)(4,1)} %bitcast.61), calls=%async_computation.8 | async-start | bytes 8388608
  373.6 5.7 %copy-start.5 = (bf16[768,256]{1,0:T(8,128)(2,1)S(1)}, bf16[768,256]{1,0:T(8,128)(2,1)}, u32[]{:S(2)}) copy-start(bf16[768,256]{1,0:T(8,128)(2,1)} %copy-done.4) | copy-start | bytes 1179652
  373.6 8.6 %slice-start.2 = ((s8[5505024]{0:T(1024)(128)(4,1)}), s8[4194304]{0:T(1024)(128)(4,1)S(1)}, s32[]{:S(2)}) async-start(s8[5505024]{0:T(1024)(128)(4,1)} %bitcast.63), calls=%async_computation.9 | async-start | bytes 8388608
  379.2 2.9 slice-start.3
  379.3 2.9 copy-start.10
  379.3 2.9 copy-start.11
Sparse Core Ops, SparseCore 0:
  46.9 84.0 all-gather.4
  134.2 84.9 all-gather.2
  257.4 109.2 reduce-scatter.1
where the time goes:
time: 411 us; the launch traced here: 410 us
  waiting for transfers between devices  238 us (58%)
  blocking collectives  61.4 us (15%)
  local copies, waits for them, and re-layouts  54.1 us (13%)
  matrix products  31.5 us (8%)
  between operations  14 us (3%)
  starting transfers between devices  9.14 us (2%)
    reduce_scatter x1, waiting for transfers between devices, per_device(): summed = lax.psum_scatter(sent_back, 'dp', scatter_dimension=0, tiled=True)  109 us
    all_gather x1, waiting for transfers between devices, per_device(): recv_scaled = lax.all_gather(sent_scaled, 'dp', axis=0, tiled=True)  62.9 us
    all_gather x1, waiting for transfers between devices, per_device(): recv_inputs = lax.all_gather(sent_inputs, 'dp', axis=0, tiled=True)  46.7 us
    all_to_all x1, blocking collectives, per_device(): sent_inputs = lax.all_to_all(input_slots, 'expert', 0, 0, tiled=True)  33.6 us
    all_to_all x1, blocking collectives, per_device(): sent_scaled = lax.all_to_all(scaled_slots, 'expert', 0, 0, tiled=True)  27.8 us
    all_to_all x1, waiting for transfers between devices, per_device(): returned = lax.all_to_all(summed, 'expert', 0, 0, tiled=True)  14.9 us
    reshape x1, local copies, waits for them, and re-layouts, per_device(): input_rows = recv_inputs.reshape(-1, model_width)  9.45 us
    reshape x1, local copies, waits for them, and re-layouts, per_device(): scaled_rows = recv_scaled.reshape(-1, model_width)  9.34 us
  transfers between devices with their start and end apart: 5, of which 5 were waited for; matrix products, arithmetic and copies ran while one was open for 10% of the time, Pallas kernels for 0%

commit v1 on v0

--- a/solution.py
+++ b/solution.py
@@ -1,7 +1,16 @@
+import functools
 import jax
 import jax.numpy as jnp
 from jax import lax
 from jax.sharding import PartitionSpec as P
+
+
+def find_frame(original, link_axis, join_dim):
+    back = jnp.stack(tuple((original for _ in range(lax.axis_size(link_axis)))))
+    return jnp.concatenate(lax.all_to_all(back, link_axis, 0, 0), axis=join_dim)
+
+
+fill_pairs_all = functools.partial(find_frame, link_axis="dp", join_dim=0)
 
 
 def passed_along(x, axis, by):
@@ -81,7 +90,7 @@
     recv_inputs = lax.all_gather(sent_inputs, "dp", axis=0, tiled=True)
     scaled_slots = by_expert((slot_weight[:, :, None] * to_slots(upstream)).astype(jnp.bfloat16))
     sent_scaled = lax.all_to_all(scaled_slots, "expert", 0, 0, tiled=True)
-    recv_scaled = lax.all_gather(sent_scaled, "dp", axis=0, tiled=True)
+    recv_scaled = fill_pairs_all(sent_scaled)
     input_rows = recv_inputs.reshape(-1, model_width)
     scaled_rows = recv_scaled.reshape(-1, model_width)
     gate_slice = w_gate[0, 0]

time: 411 us -> 389 us (0.946)
  waiting for transfers between devices: 238 us -> 126 us
  blocking collectives: 61.4 us -> 159 us
  local copies, waits for them, and re-layouts: 54.1 us -> 49.6 us
    all_to_all x0 -> x1, blocking collectives: none -> 97.4 us  [find_frame(): return jnp.concatenate(lax.all_to_all(back, link_axis, 0, 0), axis=join_dim)]
    all_gather x1 -> x0, waiting for transfers between devices: 62.9 us -> none  [per_device(): recv_scaled = lax.all_gather(sent_scaled, 'dp', axis=0, tiled=True)]
    all_gather x1, waiting for transfers between devices: 46.7 us -> 0.01 us  [per_device(): recv_inputs = lax.all_gather(sent_inputs, 'dp', axis=0, tiled=True)]
    another operation x0 -> x2, local copies, waits for them, and re-layouts: none -> 9.82 us  [the longest x1 9.36 us: per_device(): scaled_rows = recv_scaled.reshape(-1, model_width)]
    reshape x1 -> x0, local copies, waits for them, and re-layouts: 9.34 us -> none  [per_device(): scaled_rows = recv_scaled.reshape(-1, model_width)]
    all_gather x1 -> x0, local copies, waits for them, and re-layouts: 8.62 us -> none  [per_device(): recv_scaled = lax.all_gather(sent_scaled, 'dp', axis=0, tiled=True)]
    all_to_all x0 -> x1, local copies, waits for them, and re-layouts: none -> 5.03 us  [find_frame(): return jnp.concatenate(lax.all_to_all(back, link_axis, 0, 0), axis=join_dim)]
  transfers between devices with their start and end apart: 5 -> 4, of which waited for: 5 -> 3; matrix products, arithmetic and copies ran while one was open for 10% -> 7% of each run, Pallas kernels for 0% -> 0%
where the time goes in v1:
time: 389 us; the launch traced here: 388 us
  blocking collectives  159 us (41%)
  waiting for transfers between devices  126 us (32%)
  local copies, waits for them, and re-layouts  49.6 us (13%)
  matrix products  29.3 us (8%)
  between operations  14.4 us (4%)
  starting transfers between devices  8.93 us (2%)
    reduce_scatter x1, waiting for transfers between devices, per_device(): summed = lax.psum_scatter(sent_back, 'dp', scatter_dimension=0, tiled=True)  107 us
    all_to_all x1, blocking collectives, find_frame(): return jnp.concatenate(lax.all_to_all(back, link_axis, 0, 0), axis=join_dim)  97.4 us
    all_to_all x1, blocking collectives, per_device(): sent_inputs = lax.all_to_all(input_slots, 'expert', 0, 0, tiled=True)  33.6 us
    all_to_all x1, blocking collectives, per_device(): sent_scaled = lax.all_to_all(scaled_slots, 'expert', 0, 0, tiled=True)  27.8 us
    all_to_all x1, waiting for transfers between devices, per_device(): returned = lax.all_to_all(summed, 'expert', 0, 0, tiled=True)  14.9 us
    another operation x1, local copies, waits for them, and re-layouts, per_device(): scaled_rows = recv_scaled.reshape(-1, model_width)  9.36 us
    reshape x1, local copies, waits for them, and re-layouts, per_device(): input_rows = recv_inputs.reshape(-1, model_width)  9.35 us
    reshape x1, local copies, waits for them, and re-layouts, per_device(): sent_back = partial_rows.astype(jnp.bfloat16).reshape(recv_inputs.shape)  9.26 us
  transfers between devices with their start and end apart: 4, of which 3 were waited for; matrix products, arithmetic and copies ran while one was open for 7% of the time, Pallas kernels for 0%

profile of v1, /device:TPU:1, one launch (start us, length us, event | category | flops | bytes accessed | tf_op | source)
XLA Modules:
  0.0 388.3 jit_solution(7210610336454479202)
XLA Ops:
  9.5 1.3 convolution_convert_fusion.3
  11.9 33.6 %all_to_all.20 = bf16[8,12,3584]{2,1,0:T(8,128)(2,1)S(1)} all-to-all(bf16[8,12,3584]{2,1,0:T(8,128)(2,1)S(1)} %copy.71), channel_id=1, replica_groups=mesh['section'=4,'dp'=8,'expert'=8] {'expert'}, dimensions={0} | all-to-all | bytes 1376256 | tf_op jit(solution)/shard_map/all_to_all | solution.py:89
  45.5 1.2 copy.72
  46.8 2.1 collective-permute-start
  49.3 4.5 %collective-permute-done = bf16[1,2,16,3584]{3,2,1,0:T(8,128)(2,1)S(1)} collective-permute-done((bf16[1,2,16,3584]{3,2,1,0:T(8,128)(2,1)S(1)}, bf16[1,2,16,3584]{3,2,1,0:T(8,128)(2,1)S(1)}, u32[]{:S(2)}, u32[]{:S(2)}) %collective-permute-start) | collective-permute-done | bytes 229408 | tf_op jit(solution)/shard_map/ppermute | solution.py:18
  55.2 27.8 %all_to_all.21 = bf16[8,12,3584]{2,1,0:T(8,128)(2,1)S(1)} all-to-all(bf16[8,12,3584]{2,1,0:T(8,128)(2,1)S(1)} %copy.66), channel_id=1, replica_groups=mesh['section'=4,'dp'=8,'expert'=8] {'expert'}, dimensions={0} | all-to-all | bytes 1376256 | tf_op jit(solution)/shard_map/all_to_all | solution.py:92
  83.8 97.4 %all_to_all.22 = bf16[8,8,12,3584]{3,1,2,0:T(8,128)(2,1)S(1)} all-to-all(bf16[8,8,12,3584]{3,1,2,0:T(8,128)(2,1)S(1)} %stack.2), channel_id=1, replica_groups=mesh['section'=4,'dp'=8,'expert'=8] {'dp'}, dimensions={0} | all-to-all | bytes 11010048 | tf_op jit(solution)/shard_map/all_to_all | solution.py:10
  181.3 5.0 %copy.68 = bf16[8,8,12,3584]{3,2,1,0:T(8,128)(2,1)} copy(bf16[8,8,12,3584]{3,1,2,0:T(8,128)(2,1)S(1)} %all_to_all.22) | data formatting | bytes 11010048 | tf_op jit(solution)/shard_map/all_to_all | solution.py:10
  186.3 9.4 %reshape_reshape.3 = bf16[768,3584]{1,0:T(8,128)(2,1)} reshape(bf16[8,8,12,3584]{3,2,1,0:T(8,128)(2,1)} %copy.68) | data formatting | bytes 11010048 | tf_op jit(solution)/shard_map/reshape;reshape | solution.py:95
  195.7 8.6 %copy.73 = bf16[64,12,3584]{2,1,0:T(8,128)(2,1)} copy(bf16[64,12,3584]{2,0,1:T(8,128)(2,1)} %all-gather.2.cloned.1.call-done) | data formatting | bytes 11010048 | tf_op jit(solution)/shard_map/all_gather | solution.py:90
  204.3 9.4 %reshape.56 = bf16[768,3584]{1,0:T(8,128)(2,1)} reshape(bf16[64,12,3584]{2,1,0:T(8,128)(2,1)} %copy.73) | data formatting | bytes 11010048 | tf_op jit(solution)/shard_map/reshape | solution.py:94
  213.7 4.3 %fusion.6 = f32[768,256]{1,0:T(8,128)S(1)} fusion(bf16[768,3584]{1,0:T(8,128)(2,1)} %reshape.56, bf16[1,1,3584,256]{3,2,1,0:T(8,128)(2,1)S(1)} %copy-done), kind=kOutput, calls=%fused_computation.12 | convolution fusion | flops 1409286144 | bytes 8126464 | tf_op jit(solution)/shard_map/dot_general | solution.py:24
  218.0 3.5 fusion.9
  221.6 1.8 multiply_convert_fusion.1
  223.4 1.6 fusion.4
  225.2 4.0 %add_convert_fusion = bf16[768,3584]{1,0:T(8,128)(2,1)} fusion(f32[768,3584]{1,0:T(8,128)S(1)} %fusion.4, bf16[768,256]{1,0:T(8,128)(2,1)S(1)} %get-tuple-element.4, bf16[1,1,3584,256]{3,2,1,0:T(8,128)(2,1)S(1)} %copy-done.2), kind=kOutput, calls=%fused_computation | convolution fusion | flops 1414791168 | bytes 18743296 | tf_op jit(solution)/shard_map/dot_general | solution.py:48
  229.2 9.3 %reshape.57 = bf16[64,12,3584]{2,1,0:T(8,128)(2,1)} reshape(bf16[768,3584]{1,0:T(8,128)(2,1)} %add_convert_fusion) | data formatting | bytes 11010048 | tf_op jit(solution)/shard_map/reshape | solution.py:102
  238.5 106.6 %reduce-scatter.2.cloned.1.call-done = bf16[8,12,3584]{2,1,0:T(8,128)(2,1)} async-done(((bf16[64,12,3584]{2,1,0:T(8,128)(2,1)}), bf16[8,12,3584]{2,1,0:T(8,128)(2,1)}) %reduce-scatter.2.cloned.1.call-update) | async-done | bytes 688144 | tf_op jit(solution)/shard_map/reduce_scatter | solution.py:103
  345.0 6.7 %all-to-all-start.3 = ((bf16[8,12,3584]{2,1,0:T(8,128)(2,1)}), bf16[8,12,3584]{2,1,0:T(8,128)(2,1)}, u32[]{:S(2)}, u32[]{:S(2)}) async-start(bf16[8,12,3584]{2,1,0:T(8,128)(2,1)} %reduce-scatter.2.cloned.1.call-done), calls=%async_computation.4 | async-start | bytes 1835008 | tf_op jit(solution)/shard_map/all_to_all | solution.py:104
  351.8 5.6 %fusion.1 = bf16[1,1,3584,256]{3,2,1,0:T(8,128)(2,1)} fusion(bf16[768,3584]{1,0:T(8,128)(2,1)} %reshape.56, bf16[768,256]{1,0:T(8,128)(2,1)} %copy-done.5), kind=kOutput, calls=%fused_computation.5 | convolution fusion | flops 1410203648 | bytes 7733248 | tf_op jit(solution)/shard_map/dot_general | solution.py:42
  357.5 2.9 fusion
  360.4 2.9 fusion.2
  363.3 14.9 %all-to-all-done.3 = bf16[8,12,3584]{2,1,0:T(8,128)(2,1)} async-done(((bf16[8,12,3584]{2,1,0:T(8,128)(2,1)}), bf16[8,12,3584]{2,1,0:T(8,128)(2,1)}, u32[]{:S(2)}, u32[]{:S(2)}) %all-to-all-start.3) | async-done | bytes 688160 | tf_op jit(solution)/shard_map/all_to_all | solution.py:104
  378.3 1.6 copy.74
  (70 shorter events, 7.8 us)
Async XLA Ops:
  7.2 206.5 %copy-start = (bf16[1,1,3584,256]{3,2,1,0:T(8,128)(2,1)S(1)}, bf16[1,1,3584,256]{3,2,1,0:T(8,128)(2,1)}, u32[]{:S(2)}) copy-start(bf16[1,1,3584,256]{3,2,1,0:T(8,128)(2,1)} %param.11) | copy-start | bytes 5505028
  7.2 39.7 %copy-start.8 = (bf16[1,2,16,3584]{3,2,1,0:T(8,128)(2,1)S(1)}, bf16[1,2,16,3584]{3,2,1,0:T(8,128)(2,1)}, u32[]{:S(2)}) copy-start(bf16[1,2,16,3584]{3,2,1,0:T(8,128)(2,1)} %param.7) | copy-start | bytes 688132
  7.2 41.8 %copy-start.6 = (f32[1,2,16,2]{2,3,1,0:T(2,128)S(1)}, f32[1,2,16,2]{2,3,1,0:T(2,128)}, u32[]{:S(2)}) copy-start(f32[1,2,16,2]{2,3,1,0:T(2,128)} %param.10) | copy-start | bytes 772
  7.2 188.5 %all-gather.2.cloned.1.call-start = ((), (), s32[]{:S(2)}) async-start(), calls=%async_computation.5 | async-start | bytes 6193152 | tf_op jit(solution)/shard_map/all_gather | solution.py:90
  46.8 298.3 %reduce-scatter.2.cloned.1.call-start = ((), (), s32[]{:S(2)}) async-start(), calls=%async_computation.6 | async-start | bytes 8257536 | tf_op jit(solution)/shard_map/reduce_scatter | solution.py:103
  46.8 6.9 %collective-permute-start = (bf16[1,2,16,3584]{3,2,1,0:T(8,128)(2,1)S(1)}, bf16[1,2,16,3584]{3,2,1,0:T(8,128)(2,1)S(1)}, u32[]{:S(2)}, u32[]{:S(2)}) collective-permute-start(bf16[1,2,16,3584]{3,2,1,0:T(8,128)(2,1)S(1)} %copy-done.8), channel_id=1, source_target_pairs={{0,192},{64,0},{128,64},{192,128},{1,193},{65,1},{129,65},{193,129... | collective-permute-start | bytes 688136 | tf_op jit(solution)/shard_map/ppermute | solution.py:18
  213.7 4.3 %copy-start.1 = (bf16[768,3584]{1,0:T(8,128)(2,1)S(1)}, bf16[768,3584]{1,0:T(8,128)(2,1)}, u32[]{:S(2)}) copy-start(bf16[768,3584]{1,0:T(8,128)(2,1)} %reshape.56) | copy-start | bytes 16515076
  213.7 7.8 %slice-start = ((s8[5505024]{0:T(1024)(128)(4,1)}), s8[4194304]{0:T(1024)(128)(4,1)S(1)}, s32[]{:S(2)}) async-start(s8[5505024]{0:T(1024)(128)(4,1)} %bitcast.61), calls=%async_computation.7 | async-start | bytes 8388608
  218.0 5.3 %copy-start.9 = (f32[768,256]{1,0:T(8,128)}, f32[768,256]{1,0:T(8,128)S(1)}, u32[]{:S(2)}) copy-start(f32[768,256]{1,0:T(8,128)S(1)} %fusion.6) | copy-start | bytes 2359300
  218.0 3.5 slice-start.1
  218.0 3.5 copy-start.7
  221.5 1.8 copy-start.11
  223.3 1.7 copy-start.3
  223.4 1.7 copy-start.5
  223.4 1.8 copy-start.2
  238.4 119.0 %slice-start.4 = ((s8[5505024]{0:T(1024)(128)(4,1)}), s8[1310720]{0:T(1024)(128)(4,1)S(1)}, s32[]{:S(2)}) async-start(s8[5505024]{0:T(1024)(128)(4,1)} %bitcast.65), calls=%async_computation.11 | async-start | bytes 2621440
  345.0 33.2 %all-to-all-start.3 = ((bf16[8,12,3584]{2,1,0:T(8,128)(2,1)}), bf16[8,12,3584]{2,1,0:T(8,128)(2,1)}, u32[]{:S(2)}, u32[]{:S(2)}) async-start(bf16[8,12,3584]{2,1,0:T(8,128)(2,1)} %reduce-scatter.2.cloned.1.call-done), calls=%async_computation.4 | async-start | bytes 1835008 | tf_op jit(solution)/shard_map/all_to_all | solution.py:104
  351.8 5.7 %slice-start.5 = ((s8[5505024]{0:T(1024)(128)(4,1)}), s8[4194304]{0:T(1024)(128)(4,1)S(1)}, s32[]{:S(2)}) async-start(s8[5505024]{0:T(1024)(128)(4,1)} %bitcast.65), calls=%async_computation.12 | async-start | bytes 8388608
  351.8 5.7 %copy-start.4 = (bf16[768,256]{1,0:T(8,128)(2,1)S(1)}, bf16[768,256]{1,0:T(8,128)(2,1)}, u32[]{:S(2)}) copy-start(bf16[768,256]{1,0:T(8,128)(2,1)} %copy-done.3) | copy-start | bytes 1179652
  351.8 8.6 %slice-start.2 = ((s8[5505024]{0:T(1024)(128)(4,1)}), s8[4194304]{0:T(1024)(128)(4,1)S(1)}, s32[]{:S(2)}) async-start(s8[5505024]{0:T(1024)(128)(4,1)} %bitcast.63), calls=%async_computation.9 | async-start | bytes 8388608
  357.5 2.9 slice-start.3
  357.5 2.9 copy-start.10
  357.5 2.9 copy-start.12
Sparse Core Ops, SparseCore 0:
  46.9 115.8 all-gather.1
  238.6 106.4 reduce-scatter.1
